TPU v7x, 32 devices: a whole 2x2x4 slice. The times are simulated.
32 devices in a mesh: section: 2 (over core), fsdp: 2 (over y), expert: 8 (over z, x).
Axes of the slice: x: 2, y: 2, z: 4, core: 2. Of those that a mesh axis runs over, the one named last changes fastest.
Arguments:
- tokens: bfloat16 [2048, 2048], P(('fsdp', 'expert')), may hold values from -40 to 40
- norm_gain: float32 [2, 2048], P('section'), may hold values from 0.5 to 1.5
- router: bfloat16 [2, 2048, 32], P('section'), may hold values from -0.3125 to 0.3125
- w_gate: bfloat16 [2, 32, 2048, 768], P('section', 'expert', 'fsdp'), may hold values from -0.125 to 0.125
- w_up: bfloat16 [2, 32, 2048, 768], P('section', 'expert', 'fsdp'), may hold values from -0.125 to 0.125
- w_down: bfloat16 [2, 32, 768, 2048], P('section', 'expert', None, 'fsdp'), may hold values from -0.21875 to 0.21875
- routes: int32 [2, 2048, 6], P('section', ('fsdp', 'expert')), may hold values from 0 to 31, all different within a row; in each aligned block of 64 rows (0 to 63, 64 to 127, ..., all dimensions but the last counted through in order) at most 14 rows name the same one
Outputs:
- final_out: bfloat16 [2048, 2048], P(('fsdp', 'expert'), 'section')
- layer_stats: float32 [2], P('section')
Inputs may be any that keep to these rules, and one draw needn't show every extreme that they name: `routes`: each row names 6 different experts; in every aligned block of 64 rows of one layer no expert is named by more than 14 rows, a bound that some block reaches.
All inputs are finite; a program needn't handle non-finite values.
Results may differ from a plain program's by a relative error of at most 0.0065.
Values may be sent and summed in bfloat16 or wider, within the bound.
No kernel may reach another device: no remote copies, remote signals or barrier semaphores. Data moves between devices by JAX's collectives and lax.ppermute only.
A program may use at most 192 MiB of HBM per device.

v0:
```python
import jax
import jax.numpy as jnp
from jax import lax
from jax.sharding import PartitionSpec as P

TOP = 6
BLOCK = 64
epsilon = 1e-06


def other_section(value):
    return lax.ppermute(value, "section", [(0, 1), (1, 0)])


def rms_scaled(hidden_rows, gain_row):
    values = hidden_rows.astype(jnp.float32)
    scale = lax.rsqrt(jnp.mean(values * values, axis=-1, keepdims=True) + epsilon)
    return (values * scale * gain_row).astype(jnp.bfloat16)


def gate_weights(normed, router_weight, route_rows):
    logits = jnp.dot(normed, router_weight, preferred_element_type=jnp.float32)
    scores = jax.nn.sigmoid(logits)
    expert_ids = jnp.arange(router_weight.shape[1], dtype=jnp.int32)
    chosen_mask = (route_rows[:, :, None] == expert_ids[None, None, :]).astype(jnp.float32)
    chosen = jnp.sum(scores[:, None, :] * chosen_mask, axis=2)
    return chosen / jnp.sum(chosen, axis=1, keepdims=True)


def slot_positions(route_rows, experts_count, capacity):
    flat_routes = route_rows.reshape(-1)
    onehot = (flat_routes[:, None] == jnp.arange(experts_count, dtype=jnp.int32)[None, :]).astype(
        jnp.int32
    )
    before = jnp.cumsum(onehot, axis=0) - onehot
    slot_index = jnp.sum(before * onehot, axis=1)
    return (flat_routes * capacity + slot_index).reshape(route_rows.shape)


def expert_layer(entering, route_rows, gain_row, router_weight, weights, capacity):
    gate_w, up_w, down_w = weights
    width = entering.shape[1]
    experts_count = router_weight.shape[1]
    local_experts, chunk, hidden_units = gate_w.shape
    fsdp_count = lax.axis_size("fsdp")
    expert_devices = lax.axis_size("expert")
    peers = fsdp_count * expert_devices
    normed = rms_scaled(entering, gain_row)
    mix_weights = gate_weights(normed, router_weight, route_rows)
    positions = slot_positions(route_rows, experts_count, capacity)
    slot_ids = jnp.arange(experts_count * capacity, dtype=jnp.int32)
    placing = jnp.any(positions[None, :, :] == slot_ids[:, None, None], axis=2).astype(jnp.bfloat16)
    buffer = jnp.dot(placing, normed, preferred_element_type=jnp.float32).astype(jnp.bfloat16)
    outgoing = (
        buffer.reshape(expert_devices, local_experts * capacity, fsdp_count, chunk)
        .transpose(2, 0, 1, 3)
        .reshape(peers, local_experts * capacity, chunk)
    )
    arrived = lax.all_to_all(outgoing, ("fsdp", "expert"), 0, 0, tiled=True)
    arrived = arrived.reshape(peers, local_experts, capacity, chunk)
    gate_part = jnp.einsum("sjcd,jdh->sjch", arrived, gate_w, preferred_element_type=jnp.float32)
    up_part = jnp.einsum("sjcd,jdh->sjch", arrived, up_w, preferred_element_type=jnp.float32)
    both = jnp.concatenate([gate_part, up_part], axis=-1)
    summed = lax.psum_scatter(both, "fsdp", scatter_dimension=0, tiled=True)
    gate_sum = summed[..., :hidden_units]
    up_sum = summed[..., hidden_units:]
    inner_act = (jax.nn.silu(gate_sum) * up_sum).astype(jnp.bfloat16)
    inner_all = lax.all_gather(inner_act, "fsdp", axis=0, tiled=True)
    produced = jnp.einsum(
        "sjch,jhd->sjcd", inner_all, down_w, preferred_element_type=jnp.float32
    ).astype(jnp.bfloat16)
    returned = lax.all_to_all(
        produced.reshape(peers, local_experts * capacity, chunk),
        ("fsdp", "expert"),
        0,
        0,
        tiled=True,
    )
    flat_out = (
        returned.reshape(fsdp_count, expert_devices, local_experts * capacity, chunk)
        .transpose(1, 2, 0, 3)
        .reshape(experts_count * capacity, width)
    )
    picked = jnp.take(flat_out, positions, axis=0)
    branch_sum = jnp.sum(mix_weights[:, :, None] * picked.astype(jnp.float32), axis=1)
    return (entering.astype(jnp.float32) + branch_sum).astype(jnp.bfloat16)


def body(tokens, norm_gain, router, w_gate, w_up, w_down, routes):
    section_index = lax.axis_index("section")
    sections = lax.axis_size("section")
    token_rows, width = tokens.shape
    piece = token_rows // sections
    experts_count = router.shape[2]
    block_capacity = (7 * BLOCK * TOP + 6 * experts_count - 1) // (6 * experts_count)
    capacity = block_capacity * (piece // BLOCK)
    own_weights = (w_gate[0], w_up[0], w_down[0])
    other_weights = tuple((other_section(w) for w in own_weights))
    own_small = (norm_gain[0], router[0], routes[0])
    other_small = tuple((other_section(v) for v in own_small))
    hidden = lax.dynamic_slice_in_dim(tokens, section_index * piece, piece, 0)
    squares = []
    for layer in range(sections):
        mine = section_index == layer
        gain_row, router_weight, route_all = [
            jnp.where(mine, a, b) for a, b in zip(own_small, other_small)
        ]
        weights = tuple((jnp.where(mine, a, b) for a, b in zip(own_weights, other_weights)))
        route_rows = lax.dynamic_slice_in_dim(route_all, section_index * piece, piece, 0)
        hidden = expert_layer(hidden, route_rows, gain_row, router_weight, weights, capacity)
        values = hidden.astype(jnp.float32)
        squares.append(jnp.sum(values * values))
    totals = lax.psum(jnp.stack(squares), ("section", "fsdp", "expert"))
    token_total = token_rows * lax.axis_size("fsdp") * lax.axis_size("expert")
    stats = jnp.sqrt(totals / (token_total * width))
    layer_stats = lax.dynamic_slice_in_dim(stats, section_index, 1, 0)
    half_width = width // 2
    keep = lax.dynamic_slice_in_dim(hidden, section_index * half_width, half_width, 1)
    send = lax.dynamic_slice_in_dim(hidden, (1 - section_index) * half_width, half_width, 1)
    arrived = other_section(send)
    final_out = jnp.where(
        section_index == 0,
        jnp.concatenate([keep, arrived], axis=0),
        jnp.concatenate([arrived, keep], axis=0),
    )
    return (final_out, layer_stats)


def solution(mesh):
    in_specs = (
        P(("fsdp", "expert"), None),
        P("section", None),
        P("section", None, None),
        P("section", "expert", "fsdp", None),
        P("section", "expert", "fsdp", None),
        P("section", "expert", None, "fsdp"),
        P("section", ("fsdp", "expert"), None),
    )
    out_specs = (P(("fsdp", "expert"), "section"), P("section"))
    return jax.shard_map(body, mesh=mesh, in_specs=in_specs, out_specs=out_specs, check_vma=False)
```

profile of v0, /device:TPU:0, one launch (start us, length us, event | category | flops | bytes accessed | tf_op | source)
XLA Modules:
  0.0 542.5 jit_solution(15079160899732492798)
XLA Ops:
  10.1 7.8 %collective-permute-done = s32[128,6]{0,1:T(8,128)S(1)} collective-permute-done((s32[128,6]{0,1:T(8,128)S(1)}, s32[128,6]{0,1:T(8,128)S(1)}, u32[]{:S(2)}, u32[]{:S(2)}) %collective-permute-start) | collective-permute-done | bytes 3104 | tf_op jit(solution)/shard_map/ppermute | solution.py:12
  21.4 2.9 convolution_convert_fusion.1
  24.3 4.6 reshape.156
  29.5 52.1 %all_to_all.20 = bf16[16,56,1024]{2,1,0:T(8,128)(2,1)S(1)} all-to-all(bf16[16,56,1024]{2,1,0:T(8,128)(2,1)S(1)} %bitcast.172), channel_id=1, replica_groups=mesh['section'=2,'fsdp'=2,'expert'=8] {'fsdp','expert'}, dimensions={0} | all-to-all | bytes 3670016 | tf_op jit(solution)/shard_map/all_to_all | solution.py:59
  82.6 4.6 fusion.27
  87.1 4.6 fusion.30
  91.7 3.1 pad_maximum_fusion
  97.3 66.4 %reduce-scatter.3.cloned.1.call-done = f32[8,4,14,1536]{3,0,2,1:T(8,128)} async-done(((f32[16,4,14,1536]{3,0,2,1:T(8,128)}), f32[8,4,14,1536]{3,0,2,1:T(8,128)}) %reduce-scatter.3.cloned.1.call-update) | async-done | bytes 2752528 | tf_op jit(solution)/shard_map/reduce_scatter | solution.py:64
  163.7 3.0 fusion.43
  166.8 25.1 %all-gather.3.cloned.1.call-done = bf16[16,4,14,768]{3,0,2,1:T(8,128)(2,1)} async-done(((bf16[8,4,14,768]{3,0,2,1:T(8,128)(2,1)}), bf16[16,4,14,768]{3,0,2,1:T(8,128)(2,1)}) %all-gather.3.cloned.1.call-update) | async-done | bytes 1376272 | tf_op jit(solution)/shard_map/all_gather | solution.py:68
  191.9 4.9 fusion.24
  196.8 2.3 copy.68
  199.1 5.7 %all-to-all-start.1 = ((bf16[16,56,1024]{2,1,0:T(8,128)(2,1)}), bf16[16,56,1024]{2,1,0:T(8,128)(2,1)S(1)}, u32[]{:S(2)}, u32[]{:S(2)}) async-start(bf16[16,56,1024]{2,1,0:T(8,128)(2,1)} %copy.68), calls=%async_computation.2 | async-start | bytes 3670016 | tf_op jit(solution)/shard_map/all_to_all | solution.py:72
  209.0 39.2 %all-to-all-done.1 = bf16[16,56,1024]{2,1,0:T(8,128)(2,1)S(1)} async-done(((bf16[16,56,1024]{2,1,0:T(8,128)(2,1)}), bf16[16,56,1024]{2,1,0:T(8,128)(2,1)S(1)}, u32[]{:S(2)}, u32[]{:S(2)}) %all-to-all-start.1) | async-done | bytes 1835040 | tf_op jit(solution)/shard_map/all_to_all | solution.py:72
  250.6 2.5 gather_fusion
  254.7 4.2 multiply_reduce_fusion.1
  260.4 2.3 reshape.163
  262.7 2.0 copy.77
  264.7 49.3 %all_to_all.21 = bf16[16,56,1024]{2,1,0:T(8,128)(2,1)S(1)} all-to-all(bf16[16,56,1024]{2,1,0:T(8,128)(2,1)S(1)} %bitcast.174), channel_id=1, replica_groups=mesh['section'=2,'fsdp'=2,'expert'=8] {'fsdp','expert'}, dimensions={0} | all-to-all | bytes 3670016 | tf_op jit(solution)/shard_map/all_to_all | solution.py:59
  315.0 6.4 %fusion.36 = f32[16,4,14,768]{3,0,2,1:T(8,128)S(1)} fusion(bf16[16,4,14,1024]{3,0,2,1:T(8,128)(2,1)S(1)} %bitcast.178, bf16[4,1024,768]{2,1,0:T(8,128)(2,1)} %collective-permute-done.4, pred[]{:T(512)S(6)} %eq.124, bf16[1,4,1024,768]{3,2,1,0:T(8,128)(2,1)} %param.12), kind=kOutput, calls=%fused_computation.36 | convolution fusion | flops 1412431872 | bytes 17170432 | tf_op jit(solution)/shard_map/sjcd,jdh->sjch/dot_general | solution.py:61
  321.4 6.4 %fusion.39 = f32[16,4,14,768]{3,0,2,1:T(8,128)S(1)} fusion(bf16[16,4,14,1024]{3,0,2,1:T(8,128)(2,1)S(1)} %bitcast.179, bf16[4,1024,768]{2,1,0:T(8,128)(2,1)} %collective-permute-done.5, pred[]{:T(512)S(6)} %eq.124, bf16[1,4,1024,768]{3,2,1,0:T(8,128)(2,1)} %param.13), kind=kOutput, calls=%fused_computation.37 | convolution fusion | flops 1412431872 | bytes 17170432 | tf_op jit(solution)/shard_map/sjcd,jdh->sjch/dot_general | solution.py:62
  327.8 3.1 pad_maximum_fusion.1
  331.0 66.3 %reduce-scatter.5.cloned.1.call-done = f32[8,4,14,1536]{3,0,2,1:T(8,128)} async-done(((f32[16,4,14,1536]{3,0,2,1:T(8,128)}), f32[8,4,14,1536]{3,0,2,1:T(8,128)}) %reduce-scatter.5.cloned.1.call-update) | async-done | bytes 2752528 | tf_op jit(solution)/shard_map/reduce_scatter | solution.py:64
  397.3 3.0 fusion.42
  400.3 25.1 %all-gather.5.cloned.1.call-done = bf16[16,4,14,768]{3,0,2,1:T(8,128)(2,1)} async-done(((bf16[8,4,14,768]{3,0,2,1:T(8,128)(2,1)}), bf16[16,4,14,768]{3,0,2,1:T(8,128)(2,1)}) %all-gather.5.cloned.1.call-update) | async-done | bytes 1376272 | tf_op jit(solution)/shard_map/all_gather | solution.py:68
  425.5 6.7 %fusion.33 = bf16[4,1024,16,14]{1,2,3,0:T(8,128)(2,1)S(1)} fusion(bf16[16,4,14,768]{3,0,2,1:T(8,128)(2,1)} %all-gather.5.cloned.1.call-done, bf16[4,768,1024]{2,1,0:T(8,128)(2,1)} %collective-permute-done.3, pred[]{:T(512)S(6)} %eq.124, bf16[1,4,768,1024]{3,2,1,0:T(8,128)(2,1)} %param.14), kind=kOutput, calls=%fused_computation.35 | convolution fusion | flops 1413349376 | bytes 15794177 | tf_op jit(solution)/shard_map/sjch,jhd->sjcd/dot_general | solution.py:69
  432.2 2.3 copy.79
  434.4 6.0 %all-to-all-start.3 = ((bf16[16,56,1024]{2,1,0:T(8,128)(2,1)}), bf16[16,56,1024]{2,1,0:T(8,128)(2,1)S(1)}, u32[]{:S(2)}, u32[]{:S(2)}) async-start(bf16[16,56,1024]{2,1,0:T(8,128)(2,1)} %copy.79), calls=%async_computation.5 | async-start | bytes 3670016 | tf_op jit(solution)/shard_map/all_to_all | solution.py:72
  441.3 40.0 %all-to-all-done.3 = bf16[16,56,1024]{2,1,0:T(8,128)(2,1)S(1)} async-done(((bf16[16,56,1024]{2,1,0:T(8,128)(2,1)}), bf16[16,56,1024]{2,1,0:T(8,128)(2,1)S(1)}, u32[]{:S(2)}, u32[]{:S(2)}) %all-to-all-start.3) | async-done | bytes 1835040 | tf_op jit(solution)/shard_map/all_to_all | solution.py:72
  483.7 2.5 gather_fusion.1
  487.8 4.2 multiply_reduce_fusion
  494.1 39.4 %psum.7 = f32[2]{0:T(128)S(1)} all-reduce(f32[2]{0:T(128)S(1)} %pad_maximum_fusion.2), channel_id=1, replica_groups=mesh['section'=2,'fsdp'=2,'expert'=8] {'section','fsdp','expert'}, use_global_device_ids=true, to_apply=%region_20.22 | all-reduce | flops 2 | bytes 16 | tf_op jit(solution)/shard_map/psum | solution.py:113
  (103 shorter events, 30.3 us)
Async XLA Ops:
  7.2 156.6 %reduce-scatter.3.cloned.1.call-start = ((), (), s32[]{:S(2)}) async-start(), calls=%async_computation.6 | async-start | bytes 8257536 | tf_op jit(solution)/shard_map/reduce_scatter | solution.py:64
  7.2 75.3 %collective-permute-start.4 = (bf16[4,1024,768]{2,1,0:T(8,128)(2,1)}, bf16[4,1024,768]{2,1,0:T(8,128)(2,1)}, u32[]{:S(2)}, u32[]{:S(2)}) collective-permute-start(bf16[4,1024,768]{2,1,0:T(8,128)(2,1)} %bitcast.187), channel_id=1, source_target_pairs={{0,16},{16,0},{1,17},{17,1},{2,18},{18,2},{3,19},{19,3},{4,20},{20... | collective-permute-start | bytes 18874376 | tf_op jit(solution)/shard_map/ppermute | solution.py:12
  8.5 9.4 %collective-permute-start = (s32[128,6]{0,1:T(8,128)S(1)}, s32[128,6]{0,1:T(8,128)S(1)}, u32[]{:S(2)}, u32[]{:S(2)}) collective-permute-start(s32[128,6]{0,1:T(8,128)S(1)} %bitcast.186), channel_id=1, source_target_pairs={{0,16},{16,0},{1,17},{17,1},{2,18},{18,2},{3,19},{19,3},{4,20},{20... | collective-permute-start | bytes 9224 | tf_op jit(solution)/shard_map/ppermute | solution.py:12
  8.5 12.2 %collective-permute-start.1 = (f32[2048]{0:T(1024)}, f32[2048]{0:T(1024)S(1)}, u32[]{:S(2)}, u32[]{:S(2)}) collective-permute-start(f32[2048]{0:T(1024)} %bitcast.184), channel_id=1, source_target_pairs={{0,16},{16,0},{1,17},{17,1},{2,18},{18,2},{3,19},{19,3},{4,20},{20... | collective-permute-start | bytes 24584 | tf_op jit(solution)/shard_map/ppermute | solution.py:12
  9.0 78.2 %collective-permute-start.5 = (bf16[4,1024,768]{2,1,0:T(8,128)(2,1)}, bf16[4,1024,768]{2,1,0:T(8,128)(2,1)}, u32[]{:S(2)}, u32[]{:S(2)}) collective-permute-start(bf16[4,1024,768]{2,1,0:T(8,128)(2,1)} %bitcast.188), channel_id=1, source_target_pairs={{0,16},{16,0},{1,17},{17,1},{2,18},{18,2},{3,19},{19,3},{4,20},{20... | collective-permute-start | bytes 18874376 | tf_op jit(solution)/shard_map/ppermute | solution.py:12
  94.8 97.1 %all-gather.3.cloned.1.call-start = ((), (), s32[]{:S(2)}) async-start(), calls=%async_computation.7 | async-start | bytes 2064384 | tf_op jit(solution)/shard_map/all_gather | solution.py:68
  95.3 71.4 %collective-permute-start.3 = (bf16[4,768,1024]{2,1,0:T(8,128)(2,1)}, bf16[4,768,1024]{2,1,0:T(8,128)(2,1)}, u32[]{:S(2)}, u32[]{:S(2)}) collective-permute-start(bf16[4,768,1024]{2,1,0:T(8,128)(2,1)} %bitcast.189), channel_id=1, source_target_pairs={{0,16},{16,0},{1,17},{17,1},{2,18},{18,2},{3,19},{19,3},{4,20},{20... | collective-permute-start | bytes 18874376 | tf_op jit(solution)/shard_map/ppermute | solution.py:12
  199.1 5.8 %copy-start.4 = (bf16[1,2048,32]{1,2,0:T(8,128)(2,1)S(1)}, bf16[1,2048,32]{1,2,0:T(8,128)(2,1)}, u32[]{:S(2)}) copy-start(bf16[1,2048,32]{1,2,0:T(8,128)(2,1)} %param.11) | copy-start | bytes 393220
  199.1 9.5 %copy-start.2 = (bf16[128,2048]{1,0:T(8,128)(2,1)S(1)}, bf16[128,2048]{1,0:T(8,128)(2,1)}, u32[]{:S(2)}) copy-start(bf16[128,2048]{1,0:T(8,128)(2,1)} %param.9) | copy-start | bytes 1572868
  199.1 49.1 %all-to-all-start.1 = ((bf16[16,56,1024]{2,1,0:T(8,128)(2,1)}), bf16[16,56,1024]{2,1,0:T(8,128)(2,1)S(1)}, u32[]{:S(2)}, u32[]{:S(2)}) async-start(bf16[16,56,1024]{2,1,0:T(8,128)(2,1)} %copy.68), calls=%async_computation.2 | async-start | bytes 3670016 | tf_op jit(solution)/shard_map/all_to_all | solution.py:72
  204.8 192.5 %reduce-scatter.5.cloned.1.call-start = ((), (), s32[]{:S(2)}) async-start(), calls=%async_computation.8 | async-start | bytes 8257536 | tf_op jit(solution)/shard_map/reduce_scatter | solution.py:64
  204.9 3.7 collective-permute-start.2
  208.6 42.0 %copy-start.6 = (bf16[2048,32]{0,1:T(8,128)(2,1)}, bf16[2048,32]{0,1:T(8,128)(2,1)S(1)}, u32[]{:S(2)}) copy-start(bf16[2048,32]{0,1:T(8,128)(2,1)S(1)} %collective-permute-done.2) | copy-start | bytes 393220
  253.1 5.8 %copy-start.3 = (bf16[128,2048]{1,0:T(8,128)(2,1)S(1)}, bf16[128,2048]{1,0:T(8,128)(2,1)}, u32[]{:S(2)}) copy-start(bf16[128,2048]{1,0:T(8,128)(2,1)} %param.9) | copy-start | bytes 1572868
  259.7 181.1 %copy-start = (bf16[64,2048]{1,0:T(8,128)(2,1)}, bf16[64,2048]{1,0:T(8,128)(2,1)S(1)}, u32[]{:S(2)}) copy-start(bf16[64,2048]{1,0:T(8,128)(2,1)S(1)} %get-tuple-element.13) | copy-start | bytes 786436
  331.0 94.5 %all-gather.5.cloned.1.call-start = ((), (), s32[]{:S(2)}) async-start(), calls=%async_computation.9 | async-start | bytes 2064384 | tf_op jit(solution)/shard_map/all_gather | solution.py:68
  434.4 6.4 %copy-start.5 = (bf16[1,2048,32]{1,2,0:T(8,128)(2,1)S(1)}, bf16[1,2048,32]{1,2,0:T(8,128)(2,1)}, u32[]{:S(2)}) copy-start(bf16[1,2048,32]{1,2,0:T(8,128)(2,1)} %param.11) | copy-start | bytes 393220
  434.4 6.4 %copy-start.7 = (bf16[2048,32]{0,1:T(8,128)(2,1)S(1)}, bf16[2048,32]{0,1:T(8,128)(2,1)}, u32[]{:S(2)}) copy-start(bf16[2048,32]{0,1:T(8,128)(2,1)} %copy-done.6) | copy-start | bytes 393220
  434.4 46.8 %all-to-all-start.3 = ((bf16[16,56,1024]{2,1,0:T(8,128)(2,1)}), bf16[16,56,1024]{2,1,0:T(8,128)(2,1)S(1)}, u32[]{:S(2)}, u32[]{:S(2)}) async-start(bf16[16,56,1024]{2,1,0:T(8,128)(2,1)} %copy.79), calls=%async_computation.5 | async-start | bytes 3670016 | tf_op jit(solution)/shard_map/all_to_all | solution.py:72
  486.1 5.9 %copy-start.1 = (bf16[64,2048]{1,0:T(8,128)(2,1)S(1)}, bf16[64,2048]{1,0:T(8,128)(2,1)}, u32[]{:S(2)}) copy-start(bf16[64,2048]{1,0:T(8,128)(2,1)} %copy-done) | copy-start | bytes 786436
  533.6 1.4 collective-permute-start.6
Sparse Core Ops, SparseCore 0:
  94.9 68.7 reduce-scatter.2
  166.9 24.9 all-gather.2
  331.1 66.1 reduce-scatter.4
  400.5 24.9 all-gather.4
where the time goes:
time: 550 us; the launch traced here: 543 us
  waiting for transfers between devices  271 us (49%)
  blocking collectives  141 us (26%)
  matrix products  37.7 us (7%)
  local copies, waits for them, and re-layouts  32.7 us (6%)
  other arithmetic  29.4 us (5%)
  starting transfers between devices  16.7 us (3%)
  between operations  14.4 us (3%)
    reduce_scatter x2, waiting for transfers between devices, expert_layer(): summed = lax.psum_scatter(both, 'fsdp', scatter_dimension=0, tiled=True)  133 us
    all_to_all x2, blocking collectives, expert_layer(): arrived = lax.all_to_all(outgoing, ('fsdp', 'expert'), 0, 0, tiled=True)  101 us
    all_to_all x2, waiting for transfers between devices, expert_layer(): lax.all_to_all(produced.reshape(peers, local_experts * capacity, chunk),...  79.2 us
    all_gather x2, waiting for transfers between devices, expert_layer(): inner_all = lax.all_gather(inner_act, 'fsdp', axis=0, tiled=True)  50.3 us
    psum x1, blocking collectives, body(): totals = lax.psum(jnp.stack(squares), ('section', 'fsdp', 'expert'))  39.4 us
    all_to_all x2, starting transfers between devices, expert_layer(): lax.all_to_all(produced.reshape(peers, local_experts * capacity, chunk),...  11.7 us
    dot_general x2, matrix products, expert_layer(): jnp.einsum('sjch,jhd->sjcd', inner_all, down_w, preferred_element_type=jn...  11.6 us
  transfers between devices with their start and end apart: 13, of which 8 were waited for; matrix products, arithmetic and copies ran while one was open for 5% of the time, Pallas kernels for 0%

commit v1 on v0

--- a/solution.py
+++ b/solution.py
@@ -6,6 +6,28 @@
 TOP = 6
 BLOCK = 64
 epsilon = 1e-06
+
+
+def joined_along(pieces, dim):
+    shape = list(pieces.shape[1:])
+    shape[dim] *= pieces.shape[0]
+    return jnp.moveaxis(pieces, 0, dim).reshape(shape)
+
+
+def doubled(shard, axis):
+    size = lax.axis_size(axis)
+    blocks = shard[None]
+    for level in range(size.bit_length() - 1):
+        distance = 1 << level
+        other = lax.ppermute(blocks, axis, [(i, i ^ distance) for i in range(size)])
+        both = jnp.stack([blocks, other])
+        upper = lax.axis_index(axis) >> level & 1
+        blocks = jnp.where(upper == 0, both, both[::-1]).reshape(-1, *shard.shape)
+    return blocks
+
+
+def gather_by_bits(x, axis, dim):
+    return joined_along(doubled(x, axis), dim)
 
 
 def other_section(value):
@@ -65,7 +87,7 @@
     gate_sum = summed[..., :hidden_units]
     up_sum = summed[..., hidden_units:]
     inner_act = (jax.nn.silu(gate_sum) * up_sum).astype(jnp.bfloat16)
-    inner_all = lax.all_gather(inner_act, "fsdp", axis=0, tiled=True)
+    inner_all = gather_by_bits(inner_act, "fsdp", 0)
     produced = jnp.einsum(
         "sjch,jhd->sjcd", inner_all, down_w, preferred_element_type=jnp.float32
     ).astype(jnp.bfloat16)

time: 550 us -> 529 us (0.962)
  waiting for transfers between devices: 271 us -> 253 us
    all_gather x2 -> x0, waiting for transfers between devices: 50.3 us -> none  [expert_layer(): inner_all = lax.all_gather(inner_act, 'fsdp', axis=0, tiled=True)]
    ppermute x0 -> x2, waiting for transfers between devices: none -> 32.7 us  [doubled(): other = lax.ppermute(blocks, axis, [(i, i ^ distance) for i in range(size)])]
    convert_element_type x2 -> x0, other arithmetic: 6.03 us -> none  [expert_layer(): inner_act = (jax.nn.silu(gate_sum) * up_sum).astype(jnp.bfloat16)]
where the time goes in v1:
time: 529 us; the launch traced here: 525 us
  waiting for transfers between devices  253 us (48%)
  blocking collectives  140 us (26%)
  matrix products  37 us (7%)
  local copies, waits for them, and re-layouts  32.7 us (6%)
  other arithmetic  30.5 us (6%)
  starting transfers between devices  16.7 us (3%)
  between operations  14.7 us (3%)
    reduce_scatter x2, waiting for transfers between devices, expert_layer(): summed = lax.psum_scatter(both, 'fsdp', scatter_dimension=0, tiled=True)  133 us
    all_to_all x2, blocking collectives, expert_layer(): arrived = lax.all_to_all(outgoing, ('fsdp', 'expert'), 0, 0, tiled=True)  101 us
    all_to_all x2, waiting for transfers between devices, expert_layer(): lax.all_to_all(produced.reshape(peers, local_experts * capacity, chunk),...  78.1 us
    psum x1, blocking collectives, body(): totals = lax.psum(jnp.stack(squares), ('section', 'fsdp', 'expert'))  39.4 us
    ppermute x2, waiting for transfers between devices, doubled(): other = lax.ppermute(blocks, axis, [(i, i ^ distance) for i in range(size)])  32.7 us
    all_to_all x2, starting transfers between devices, expert_layer(): lax.all_to_all(produced.reshape(peers, local_experts * capacity, chunk),...  11.7 us
    dot_general x2, matrix products, expert_layer(): jnp.einsum('sjch,jhd->sjcd', inner_all, down_w, preferred_element_type=jn...  10.9 us
    dot_general x2, matrix products, expert_layer(): jnp.einsum('sjcd,jdh->sjch', arrived, up_w, preferred_element_type=jnp.fl...  10.9 us
  transfers between devices with their start and end apart: 13, of which 8 were waited for; matrix products, arithmetic and copies ran while one was open for 5% of the time, Pallas kernels for 0%

profile of v1, /device:TPU:0, one launch (start us, length us, event | category | flops | bytes accessed | tf_op | source)
XLA Modules:
  0.0 524.6 jit_solution(14855121201504157841)
XLA Ops:
  10.1 7.8 %collective-permute-done = s32[128,6]{0,1:T(8,128)S(1)} collective-permute-done((s32[128,6]{0,1:T(8,128)S(1)}, s32[128,6]{0,1:T(8,128)S(1)}, u32[]{:S(2)}, u32[]{:S(2)}) %collective-permute-start) | collective-permute-done | bytes 3104 | tf_op jit(solution)/shard_map/ppermute | solution.py:34
  21.4 2.9 convolution_convert_fusion.1
  24.3 4.6 reshape.156
  29.5 52.4 %all_to_all.20 = bf16[16,56,1024]{2,1,0:T(8,128)(2,1)S(1)} all-to-all(bf16[16,56,1024]{2,1,0:T(8,128)(2,1)S(1)} %bitcast.186), channel_id=1, replica_groups=mesh['section'=2,'fsdp'=2,'expert'=8] {'fsdp','expert'}, dimensions={0} | all-to-all | bytes 3670016 | tf_op jit(solution)/shard_map/all_to_all | solution.py:81
  82.8 4.6 fusion.27
  87.4 4.6 fusion.30
  92.0 3.1 pad_maximum_fusion
  97.1 66.9 %reduce-scatter.3.cloned.1.call-done = f32[8,4,14,1536]{3,0,2,1:T(8,128)} async-done(((f32[16,4,14,1536]{3,0,2,1:T(8,128)}), f32[8,4,14,1536]{3,0,2,1:T(8,128)}) %reduce-scatter.3.cloned.1.call-update) | async-done | bytes 2752528 | tf_op jit(solution)/shard_map/reduce_scatter | solution.py:86
  164.0 3.2 fusion.102
  167.9 16.5 %collective-permute-done.6 = bf16[1,8,4,14,768]{4,1,3,2,0:T(8,128)(2,1)S(1)} collective-permute-done((bf16[1,8,4,14,768]{4,1,3,2,0:T(8,128)(2,1)}, bf16[1,8,4,14,768]{4,1,3,2,0:T(8,128)(2,1)S(1)}, u32[]{:S(2)}, u32[]{:S(2)}) %collective-permute-start.6) | collective-permute-done | bytes 688160 | tf_op jit(solution)/shard_map/ppermute | solution.py:22
  184.8 4.6 fusion.24
  189.4 2.3 copy.75
  191.6 5.7 %all-to-all-start.1 = ((bf16[16,56,1024]{2,1,0:T(8,128)(2,1)}), bf16[16,56,1024]{2,1,0:T(8,128)(2,1)S(1)}, u32[]{:S(2)}, u32[]{:S(2)}) async-start(bf16[16,56,1024]{2,1,0:T(8,128)(2,1)} %copy.75), calls=%async_computation.2 | async-start | bytes 3670016 | tf_op jit(solution)/shard_map/all_to_all | solution.py:94
  201.3 39.1 %all-to-all-done.1 = bf16[16,56,1024]{2,1,0:T(8,128)(2,1)S(1)} async-done(((bf16[16,56,1024]{2,1,0:T(8,128)(2,1)}), bf16[16,56,1024]{2,1,0:T(8,128)(2,1)S(1)}, u32[]{:S(2)}, u32[]{:S(2)}) %all-to-all-start.1) | async-done | bytes 1835040 | tf_op jit(solution)/shard_map/all_to_all | solution.py:94
  242.8 2.5 gather_fusion
  246.8 4.3 multiply_reduce_fusion.1
  252.6 2.3 reshape.163
  254.9 2.0 copy.84
  256.9 48.5 %all_to_all.21 = bf16[16,56,1024]{2,1,0:T(8,128)(2,1)S(1)} all-to-all(bf16[16,56,1024]{2,1,0:T(8,128)(2,1)S(1)} %bitcast.188), channel_id=1, replica_groups=mesh['section'=2,'fsdp'=2,'expert'=8] {'fsdp','expert'}, dimensions={0} | all-to-all | bytes 3670016 | tf_op jit(solution)/shard_map/all_to_all | solution.py:81
  306.4 6.4 %fusion.36 = f32[16,4,14,768]{3,0,2,1:T(8,128)S(1)} fusion(bf16[16,4,14,1024]{3,0,2,1:T(8,128)(2,1)S(1)} %bitcast.192, bf16[4,1024,768]{2,1,0:T(8,128)(2,1)} %collective-permute-done.4, pred[]{:T(512)S(6)} %eq.129, bf16[1,4,1024,768]{3,2,1,0:T(8,128)(2,1)} %param.12), kind=kOutput, calls=%fused_computation.38 | convolution fusion | flops 1412431872 | bytes 17170432 | tf_op jit(solution)/shard_map/sjcd,jdh->sjch/dot_general | solution.py:83
  312.8 6.4 %fusion.39 = f32[16,4,14,768]{3,0,2,1:T(8,128)S(1)} fusion(bf16[16,4,14,1024]{3,0,2,1:T(8,128)(2,1)S(1)} %bitcast.193, bf16[4,1024,768]{2,1,0:T(8,128)(2,1)} %collective-permute-done.5, pred[]{:T(512)S(6)} %eq.129, bf16[1,4,1024,768]{3,2,1,0:T(8,128)(2,1)} %param.13), kind=kOutput, calls=%fused_computation.39 | convolution fusion | flops 1412431872 | bytes 17170432 | tf_op jit(solution)/shard_map/sjcd,jdh->sjch/dot_general | solution.py:84
  319.2 3.1 pad_maximum_fusion.1
  322.4 66.3 %reduce-scatter.5.cloned.1.call-done = f32[8,4,14,1536]{3,0,2,1:T(8,128)} async-done(((f32[16,4,14,1536]{3,0,2,1:T(8,128)}), f32[8,4,14,1536]{3,0,2,1:T(8,128)}) %reduce-scatter.5.cloned.1.call-update) | async-done | bytes 2752528 | tf_op jit(solution)/shard_map/reduce_scatter | solution.py:86
  388.7 2.3 fusion.100
  391.9 16.2 %collective-permute-done.7 = bf16[1,8,4,14,768]{4,1,3,2,0:T(8,128)(2,1)S(1)} collective-permute-done((bf16[1,8,4,14,768]{4,1,3,2,0:T(8,128)(2,1)S(1)}, bf16[1,8,4,14,768]{4,1,3,2,0:T(8,128)(2,1)S(1)}, u32[]{:S(2)}, u32[]{:S(2)}) %collective-permute-start.7) | collective-permute-done | bytes 688160 | tf_op jit(solution)/shard_map/ppermute | solution.py:22
  408.5 6.4 %fusion.33 = bf16[4,1024,16,14]{1,2,3,0:T(8,128)(2,1)S(1)} fusion(bf16[4,768,1024]{2,1,0:T(8,128)(2,1)} %collective-permute-done.3, pred[]{:T(512)S(6)} %eq.129, bf16[2,1,8,4,14,768]{5,2,4,3,1,0:T(8,128)(2,1)S(1)} %reverse_select_fusion, bf16[1,4,768,1024]{3,2,1,0:T(8,128)(2,1)} %param.14), kind=kOutput, calls=%fused_computation.37 | convolution fusion | flops 1413349376 | bytes 15794177 | tf_op jit(solution)/shard_map/sjch,jhd->sjcd/dot_general | solution.py:91
  414.9 2.3 copy.87
  417.2 6.0 %all-to-all-start.3 = ((bf16[16,56,1024]{2,1,0:T(8,128)(2,1)}), bf16[16,56,1024]{2,1,0:T(8,128)(2,1)S(1)}, u32[]{:S(2)}, u32[]{:S(2)}) async-start(bf16[16,56,1024]{2,1,0:T(8,128)(2,1)} %copy.87), calls=%async_computation.5 | async-start | bytes 3670016 | tf_op jit(solution)/shard_map/all_to_all | solution.py:94
  424.0 39.0 %all-to-all-done.3 = bf16[16,56,1024]{2,1,0:T(8,128)(2,1)S(1)} async-done(((bf16[16,56,1024]{2,1,0:T(8,128)(2,1)}), bf16[16,56,1024]{2,1,0:T(8,128)(2,1)S(1)}, u32[]{:S(2)}, u32[]{:S(2)}) %all-to-all-start.3) | async-done | bytes 1835040 | tf_op jit(solution)/shard_map/all_to_all | solution.py:94
  465.4 2.5 gather_fusion.1
  469.5 4.3 multiply_reduce_fusion
  475.9 39.4 %psum.7 = f32[2]{0:T(128)S(1)} all-reduce(f32[2]{0:T(128)S(1)} %pad_maximum_fusion.4), channel_id=1, replica_groups=mesh['section'=2,'fsdp'=2,'expert'=8] {'section','fsdp','expert'}, use_global_device_ids=true, to_apply=%region_20.22 | all-reduce | flops 2 | bytes 16 | tf_op jit(solution)/shard_map/psum | solution.py:135
  (111 shorter events, 31.8 us)
Async XLA Ops:
  7.2 156.8 %reduce-scatter.3.cloned.1.call-start = ((), (), s32[]{:S(2)}) async-start(), calls=%async_computation.6 | async-start | bytes 8257536 | tf_op jit(solution)/shard_map/reduce_scatter | solution.py:86
  7.2 75.6 %collective-permute-start.4 = (bf16[4,1024,768]{2,1,0:T(8,128)(2,1)}, bf16[4,1024,768]{2,1,0:T(8,128)(2,1)}, u32[]{:S(2)}, u32[]{:S(2)}) collective-permute-start(bf16[4,1024,768]{2,1,0:T(8,128)(2,1)} %bitcast.203), channel_id=1, source_target_pairs={{0,16},{16,0},{1,17},{17,1},{2,18},{18,2},{3,19},{19,3},{4,20},{20... | collective-permute-start | bytes 18874376 | tf_op jit(solution)/shard_map/ppermute | solution.py:34
  8.5 9.4 %collective-permute-start = (s32[128,6]{0,1:T(8,128)S(1)}, s32[128,6]{0,1:T(8,128)S(1)}, u32[]{:S(2)}, u32[]{:S(2)}) collective-permute-start(s32[128,6]{0,1:T(8,128)S(1)} %bitcast.202), channel_id=1, source_target_pairs={{0,16},{16,0},{1,17},{17,1},{2,18},{18,2},{3,19},{19,3},{4,20},{20... | collective-permute-start | bytes 9224 | tf_op jit(solution)/shard_map/ppermute | solution.py:34
  8.5 12.2 %collective-permute-start.1 = (f32[2048]{0:T(1024)}, f32[2048]{0:T(1024)S(1)}, u32[]{:S(2)}, u32[]{:S(2)}) collective-permute-start(f32[2048]{0:T(1024)} %bitcast.200), channel_id=1, source_target_pairs={{0,16},{16,0},{1,17},{17,1},{2,18},{18,2},{3,19},{19,3},{4,20},{20... | collective-permute-start | bytes 24584 | tf_op jit(solution)/shard_map/ppermute | solution.py:34
  9.0 78.4 %collective-permute-start.5 = (bf16[4,1024,768]{2,1,0:T(8,128)(2,1)}, bf16[4,1024,768]{2,1,0:T(8,128)(2,1)}, u32[]{:S(2)}, u32[]{:S(2)}) collective-permute-start(bf16[4,1024,768]{2,1,0:T(8,128)(2,1)} %bitcast.204), channel_id=1, source_target_pairs={{0,16},{16,0},{1,17},{17,1},{2,18},{18,2},{3,19},{19,3},{4,20},{20... | collective-permute-start | bytes 18874376 | tf_op jit(solution)/shard_map/ppermute | solution.py:34
  95.1 89.7 %collective-permute-start.3 = (bf16[4,768,1024]{2,1,0:T(8,128)(2,1)}, bf16[4,768,1024]{2,1,0:T(8,128)(2,1)}, u32[]{:S(2)}, u32[]{:S(2)}) collective-permute-start(bf16[4,768,1024]{2,1,0:T(8,128)(2,1)} %bitcast.205), channel_id=1, source_target_pairs={{0,16},{16,0},{1,17},{17,1},{2,18},{18,2},{3,19},{19,3},{4,20},{20... | collective-permute-start | bytes 18874376 | tf_op jit(solution)/shard_map/ppermute | solution.py:34
  164.0 3.5 copy-start
  167.2 17.2 %collective-permute-start.6 = (bf16[1,8,4,14,768]{4,1,3,2,0:T(8,128)(2,1)}, bf16[1,8,4,14,768]{4,1,3,2,0:T(8,128)(2,1)S(1)}, u32[]{:S(2)}, u32[]{:S(2)}) collective-permute-start(bf16[1,8,4,14,768]{4,1,3,2,0:T(8,128)(2,1)} %fusion.102), channel_id=1, source_target_pairs={{0,8},{8,0},{1,9},{9,1},{2,10},{10,2},{3,11},{11,3},{4,12},{12,4},... | collective-permute-start | bytes 2064392 | tf_op jit(solution)/shard_map/ppermute | solution.py:22
  191.6 6.3 %copy-start.6 = (bf16[1,2048,32]{1,2,0:T(8,128)(2,1)S(1)}, bf16[1,2048,32]{1,2,0:T(8,128)(2,1)}, u32[]{:S(2)}) copy-start(bf16[1,2048,32]{1,2,0:T(8,128)(2,1)} %param.11) | copy-start | bytes 393220
  191.6 9.2 %copy-start.4 = (bf16[128,2048]{1,0:T(8,128)(2,1)S(1)}, bf16[128,2048]{1,0:T(8,128)(2,1)}, u32[]{:S(2)}) copy-start(bf16[128,2048]{1,0:T(8,128)(2,1)} %param.9) | copy-start | bytes 1572868
  191.6 48.7 %all-to-all-start.1 = ((bf16[16,56,1024]{2,1,0:T(8,128)(2,1)}), bf16[16,56,1024]{2,1,0:T(8,128)(2,1)S(1)}, u32[]{:S(2)}, u32[]{:S(2)}) async-start(bf16[16,56,1024]{2,1,0:T(8,128)(2,1)} %copy.75), calls=%async_computation.2 | async-start | bytes 3670016 | tf_op jit(solution)/shard_map/all_to_all | solution.py:94
  197.4 191.3 %reduce-scatter.5.cloned.1.call-start = ((), (), s32[]{:S(2)}) async-start(), calls=%async_computation.7 | async-start | bytes 8257536 | tf_op jit(solution)/shard_map/reduce_scatter | solution.py:86
  198.0 2.9 collective-permute-start.2
  200.8 41.4 %copy-start.8 = (bf16[2048,32]{0,1:T(8,128)(2,1)}, bf16[2048,32]{0,1:T(8,128)(2,1)S(1)}, u32[]{:S(2)}) copy-start(bf16[2048,32]{0,1:T(8,128)(2,1)S(1)} %collective-permute-done.2) | copy-start | bytes 393220
  246.8 4.3 copy-start.5
  251.9 171.6 %copy-start.2 = (bf16[64,2048]{1,0:T(8,128)(2,1)}, bf16[64,2048]{1,0:T(8,128)(2,1)S(1)}, u32[]{:S(2)}) copy-start(bf16[64,2048]{1,0:T(8,128)(2,1)S(1)} %get-tuple-element.13) | copy-start | bytes 786436
  388.7 2.7 copy-start.1
  391.0 17.1 %collective-permute-start.7 = (bf16[1,8,4,14,768]{4,1,3,2,0:T(8,128)(2,1)S(1)}, bf16[1,8,4,14,768]{4,1,3,2,0:T(8,128)(2,1)S(1)}, u32[]{:S(2)}, u32[]{:S(2)}) collective-permute-start(bf16[1,8,4,14,768]{4,1,3,2,0:T(8,128)(2,1)S(1)} %fusion.100), channel_id=1, source_target_pairs={{0,8},{8,0},{1,9},{9,1},{2,10},{10,2},{3,11},{11,3},{4,12},{12,4},... | collective-permute-start | bytes 2064392 | tf_op jit(solution)/shard_map/ppermute | solution.py:22
  417.1 6.4 %copy-start.7 = (bf16[1,2048,32]{1,2,0:T(8,128)(2,1)S(1)}, bf16[1,2048,32]{1,2,0:T(8,128)(2,1)}, u32[]{:S(2)}) copy-start(bf16[1,2048,32]{1,2,0:T(8,128)(2,1)} %param.11) | copy-start | bytes 393220
  417.2 6.4 %copy-start.9 = (bf16[2048,32]{0,1:T(8,128)(2,1)S(1)}, bf16[2048,32]{0,1:T(8,128)(2,1)}, u32[]{:S(2)}) copy-start(bf16[2048,32]{0,1:T(8,128)(2,1)} %copy-done.8) | copy-start | bytes 393220
  417.2 45.9 %all-to-all-start.3 = ((bf16[16,56,1024]{2,1,0:T(8,128)(2,1)}), bf16[16,56,1024]{2,1,0:T(8,128)(2,1)S(1)}, u32[]{:S(2)}, u32[]{:S(2)}) async-start(bf16[16,56,1024]{2,1,0:T(8,128)(2,1)} %copy.87), calls=%async_computation.5 | async-start | bytes 3670016 | tf_op jit(solution)/shard_map/all_to_all | solution.py:94
  469.5 4.3 copy-start.3
  515.4 1.4 collective-permute-start.8
Sparse Core Ops, SparseCore 0:
  95.2 68.7 reduce-scatter.2
  322.5 66.1 reduce-scatter.4
